TPU v7x, 256 devices: a whole 4x4x8 slice. The times are simulated.
256 devices in a mesh: role: 2 (over core), dp: 16 (over x, y), tensor: 8 (over z).
Axes of the slice: x: 4, y: 4, z: 8, core: 2. Of those that a mesh axis runs over, the one named last changes fastest.
Arguments:
- queries: bfloat16 [1024, 128, 576], P(('dp', 'tensor'), 'role'), may hold values from -13 to 13
- latent_cache: bfloat16 [512, 1024, 576], P(('dp', 'tensor')), may hold values from -4 to 4
- new_latent: bfloat16 [1024, 576], P(('dp', 'tensor')), may hold values from -9 to 9
- cache_lengths: int32 [512], P(('dp', 'tensor')), may hold values from 2 to 1024
- value_proj: bfloat16 [128, 512, 128], P(('role', 'tensor')), may hold values from -1 to 1
- out_proj: bfloat16 [16384, 7168], P(('role', 'tensor'), 'dp'), may hold values from -0.046875 to 0.046875
- residual: bfloat16 [1024, 7168], P(('role', 'tensor'), 'dp'), may hold values from -68 to 68
- norm_gain: bfloat16 [7168], replicated, may hold values from 0.5 to 1.5
- routes: int32 [1024, 8], P(('role', 'tensor')), may hold values from 0 to 15, all different within a row; in each aligned block of 64 rows (0 to 63, 64 to 127, ...) at most 40 rows name the same one
- gate_values: float32 [1024, 8], P(('role', 'tensor')), may hold values from 0.2 to 0.8
- tenant_ids: int32 [1024], P(('role', 'tensor')), may hold values from 0 to 2
- expert_gate_weight: bfloat16 [16, 7168, 2048], P('dp', None, ('role', 'tensor')), may hold values from -0.0625 to 0.0625
- expert_up_weight: bfloat16 [16, 7168, 2048], P('dp', None, ('role', 'tensor')), may hold values from -0.0625 to 0.0625
- expert_down_weight: bfloat16 [16, 2048, 7168], P('dp', ('role', 'tensor')), may hold values from -0.125 to 0.125
- left_delta_factor: bfloat16 [3, 16, 2048, 64], P(None, 'dp', ('role', 'tensor')), may hold values from -0.125 to 0.125
- factor_right: bfloat16 [3, 16, 64, 7168], P(None, 'dp'), may hold values from -0.75 to 0.75
Outputs:
- mixed: bfloat16 [1024, 7168], P(('role', 'tensor'), 'dp')
Inputs may be any that keep to these rules, and one draw needn't show every extreme that they name: `routes`: in each aligned block of 64 tokens no expert is named by more than 40 of them.
All inputs are finite; a program needn't handle non-finite values.
Results may differ from a plain program's by a relative error of at most 0.008.
Values may be sent and summed in bfloat16 or wider, within the bound.
No kernel may reach another device: no remote copies, remote signals or barrier semaphores. Data moves between devices by JAX's collectives and lax.ppermute only.
A program may use at most 128 MiB of HBM per device.

v0:
```python
import jax
import jax.numpy as jnp
from jax import lax
from jax.sharding import PartitionSpec as P

LAT = 512
EXPERTS = 16
TEN = 3
SCORE_SCALE = 0.07216878364870323
NORM_EPS = 1e-06
MASKED = -1e30
RT = ("role", "tensor")


def rms_rows(input_rows, norm_gain):
    wide = input_rows.astype(jnp.float32)
    scale = lax.rsqrt(jnp.mean(wide * wide, axis=-1, keepdims=True) + NORM_EPS)
    return (wide * scale * norm_gain.astype(jnp.float32)).astype(jnp.bfloat16)


def slot_table(routes, expert, capacity):
    hit = jnp.any(routes == expert, axis=-1).astype(jnp.int32)
    earlier = jnp.cumsum(hit, axis=-1) - hit
    slot_ids = jnp.arange(capacity, dtype=jnp.int32)
    return (hit[..., None, :] > 0) & (earlier[..., None, :] == slot_ids[:, None])


def local(
    queries,
    latent_cache,
    new_latent,
    cache_lengths,
    value_proj,
    out_proj,
    residual,
    norm_gain,
    routes,
    gate_values,
    tenant_ids,
    expert_gate_weight,
    expert_up_weight,
    expert_down_weight,
    left_delta_factor,
    factor_right,
):
    n_slices = lax.axis_size(RT)
    slice_idx = lax.axis_index(RT)
    group_rows = residual.shape[0]
    capacity = 5 * group_rows // 8
    model_width = expert_down_weight.shape[2]
    col_width = model_width // n_slices
    expert = lax.axis_index("dp")
    labels = jnp.arange(EXPERTS, dtype=jnp.int32)
    table = slot_table(routes, labels[:, None, None], capacity)
    mine = lax.dynamic_index_in_dim(table, expert, 0, keepdims=False)
    mine_owner = jnp.sum(mine.astype(jnp.int32) * tenant_ids[None, :], axis=1)
    hidden_slice = expert_down_weight.shape[1]
    down_local = expert_down_weight[0].reshape(hidden_slice, n_slices, col_width)
    left_local = left_delta_factor[:, 0]
    tenants, _, rank = left_local.shape
    left_local = jnp.transpose(left_local, (1, 0, 2)).reshape(hidden_slice, 1, tenants * rank)
    left_local = jnp.broadcast_to(left_local, (hidden_slice, n_slices, tenants * rank))
    down_pack = jnp.concatenate([down_local, left_local], axis=2)
    pack_width = down_pack.shape[2]
    slot_token = jnp.sum(
        mine.astype(jnp.int32) * jnp.arange(group_rows, dtype=jnp.int32)[None, :], axis=1
    )
    slot_used = jnp.sum(mine.astype(jnp.int32), axis=1)
    info = jnp.concatenate([slot_token, slot_used, mine_owner]).astype(jnp.bfloat16)
    info_rows = jnp.zeros((8, pack_width), jnp.bfloat16).at[0, : info.shape[0]].set(info)
    info_rows = jnp.broadcast_to(info_rows[:, None, :], (8, n_slices, pack_width))
    down_pack = jnp.concatenate([down_pack, info_rows], axis=0)
    down_pack = lax.all_to_all(down_pack, RT, split_axis=1, concat_axis=0, tiled=True)
    right_w = lax.dynamic_slice_in_dim(factor_right[:, 0], slice_idx * col_width, col_width, 2)
    seq_count, context, width = latent_cache.shape
    local_heads = queries.shape[1]
    paired = queries.reshape(seq_count, 2, local_heads, width)
    scores = (
        jnp.einsum("sqhd,spd->sqhp", paired, latent_cache, preferred_element_type=jnp.float32)
        * SCORE_SCALE
    )
    present = jnp.arange(context, dtype=jnp.int32)[None, :] < cache_lengths[:, None]
    scores = jnp.where(present[:, None, None, :], scores, MASKED)
    fresh_keys = new_latent.reshape(seq_count, 2, width)
    fresh = (
        jnp.einsum("sqhd,skd->sqhk", paired, fresh_keys, preferred_element_type=jnp.float32)
        * SCORE_SCALE
    )
    causal = jnp.arange(2)[:, None] >= jnp.arange(2)[None, :]
    fresh = jnp.where(causal[None, :, None, :], fresh, MASKED)
    top = jnp.maximum(jnp.max(scores, axis=3), jnp.max(fresh, axis=3))[..., None]
    weights = jnp.exp(scores - top)
    fresh_weights = jnp.exp(fresh - top)
    total = jnp.sum(weights, axis=3) + jnp.sum(fresh_weights, axis=3)
    summed = jnp.einsum(
        "sqhp,spd->sqhd",
        weights.astype(jnp.bfloat16),
        latent_cache[:, :, :LAT],
        preferred_element_type=jnp.float32,
    )
    summed = summed + jnp.einsum(
        "sqhk,skd->sqhd",
        fresh_weights.astype(jnp.bfloat16),
        fresh_keys[:, :, :LAT],
        preferred_element_type=jnp.float32,
    )
    attended = (
        (summed / total[..., None]).astype(jnp.bfloat16).reshape(seq_count * 2, local_heads, LAT)
    )
    by_head = lax.all_to_all(attended, "tensor", split_axis=1, concat_axis=0, tiled=True)
    head_values = jnp.einsum(
        "thl,hlv->thv", by_head, value_proj, preferred_element_type=jnp.float32
    ).astype(jnp.bfloat16)
    head_values = head_values.reshape(
        head_values.shape[0], head_values.shape[1] * head_values.shape[2]
    )
    all_values = lax.all_gather(head_values, "dp", axis=0, tiled=True)
    down_pack, all_values = lax.optimization_barrier((down_pack, all_values))
    partial = jnp.dot(all_values, out_proj, preferred_element_type=jnp.float32)
    partial = lax.psum_scatter(partial, "role", scatter_dimension=0, tiled=True)
    attention = lax.psum_scatter(partial, "tensor", scatter_dimension=0, tiled=True)
    mixed_in = lax.optimization_barrier(
        (residual.astype(jnp.float32) + attention).astype(jnp.bfloat16)
    )
    down_pack = down_pack.reshape(n_slices, hidden_slice + 8, pack_width)
    info = down_pack[:, hidden_slice, : 3 * capacity].astype(jnp.int32)
    slot_token, slot_used, owners = (
        info[:, :capacity],
        info[:, capacity : 2 * capacity],
        info[:, 2 * capacity :],
    )
    owners = owners.reshape(n_slices * capacity)
    n_cols = lax.axis_size("dp")
    everything = lax.all_gather(mixed_in, ("role", "tensor", "dp"), axis=0, tiled=True)
    everything = everything.reshape(n_slices, n_cols, group_rows, mixed_in.shape[1])
    one_hot = (slot_token[:, :, None] == jnp.arange(group_rows, dtype=jnp.int32)[None, None, :]) & (
        slot_used[:, :, None] > 0
    )
    picked = jnp.einsum(
        "ncg,ndgk->ncdk",
        one_hot.astype(jnp.bfloat16),
        everything,
        preferred_element_type=jnp.float32,
    )
    picked = picked.reshape(n_slices * capacity, model_width)
    scale = lax.rsqrt(jnp.mean(picked * picked, axis=-1, keepdims=True) + NORM_EPS)
    collected_rows = (picked * scale * norm_gain.astype(jnp.float32)).astype(jnp.bfloat16)
    gate_scores = jnp.dot(collected_rows, expert_gate_weight[0], preferred_element_type=jnp.float32)
    upper_bound = jnp.dot(collected_rows, expert_up_weight[0], preferred_element_type=jnp.float32)
    hidden = (jax.nn.silu(gate_scores) * upper_bound).astype(jnp.bfloat16)
    gathered = lax.all_gather(hidden, RT, axis=0, tiled=False)
    hidden_all = jnp.transpose(gathered, (1, 0, 2)).reshape(hidden.shape[0], -1)
    down_pack = down_pack[:, :hidden_slice].reshape(n_slices * hidden_slice, pack_width)
    down_w = down_pack[:, :col_width]
    left_w = down_pack[:, col_width:].reshape(n_slices * hidden_slice, tenants, rank)
    base_output = jnp.dot(hidden_all, down_w, preferred_element_type=jnp.float32)
    owner_mask = (owners[:, None] == jnp.arange(TEN, dtype=jnp.int32)[None, :]).astype(jnp.float32)
    mixing = (
        jnp.einsum("sf,ftr->str", hidden_all, left_w, preferred_element_type=jnp.float32)
        * owner_mask[:, :, None]
    )
    delta = jnp.einsum(
        "str,trd->sd", mixing, right_w.astype(jnp.float32), precision=lax.Precision.HIGHEST
    )
    expert_out = (base_output - delta).astype(jnp.bfloat16)
    expert_out = expert_out.reshape(n_slices, capacity, col_width)
    by_group = lax.all_to_all(expert_out, RT, split_axis=0, concat_axis=0, tiled=True)
    by_expert = lax.all_to_all(by_group, "dp", split_axis=0, concat_axis=0, tiled=True)
    chosen = (routes[:, :, None] == labels[None, None, :]).astype(jnp.float32)
    gate_of = jnp.sum(gate_values[:, :, None] * chosen, axis=1)
    weighting = table.astype(jnp.float32) * gate_of.T[:, None, :]
    expert_part = jnp.einsum(
        "ecg,ecd->gd", weighting, by_expert.astype(jnp.float32), precision=lax.Precision.HIGHEST
    )
    return (mixed_in.astype(jnp.float32) + expert_part).astype(jnp.bfloat16)


def solution(mesh):
    placed = (
        P(("dp", "tensor"), "role", None),
        P(("dp", "tensor"), None, None),
        P(("dp", "tensor"), None),
        P(("dp", "tensor")),
        P(("role", "tensor"), None, None),
        P(("role", "tensor"), "dp"),
        P(("role", "tensor"), "dp"),
        P(),
        P(("role", "tensor"), None),
        P(("role", "tensor"), None),
        P(("role", "tensor")),
        P("dp", None, ("role", "tensor")),
        P("dp", None, ("role", "tensor")),
        P("dp", ("role", "tensor"), None),
        P(None, "dp", ("role", "tensor"), None),
        P(None, "dp", None, None),
    )
    return jax.shard_map(
        local, mesh=mesh, in_specs=placed, out_specs=P(("role", "tensor"), "dp"), check_vma=False
    )
```

profile of v0, /device:TPU:32, one launch (start us, length us, event | category | flops | bytes accessed | tf_op | source)
XLA Modules:
  0.0 471.5 jit_solution(3004877601197552970)
XLA Ops:
  6.5 0.9 reshape.238
  7.4 0.7 reshape.225
  8.1 0.7 iota_compare_fusion.4
  8.9 1.7 fusion.64
  10.5 3.8 fusion.7
  14.4 0.6 fusion.12
  15.0 1.7 fusion.2
  16.8 0.4 fusion.17
  17.1 1.1 copy.65
  18.3 8.7 %all-to-all-start.1 = ((bf16[8,64,512]{2,0,1:T(8,128)(2,1)}), bf16[8,64,512]{2,0,1:T(8,128)(2,1)S(1)}, u32[]{:S(2)}, u32[]{:S(2)}) async-start(bf16[8,64,512]{2,0,1:T(8,128)(2,1)} %copy.65), calls=%async_computation.1 | async-start | bytes 1048576 | tf_op jit(solution)/shard_map/all_to_all | solution.py:110
  27.0 0.2 reduce_window_sum.11
  27.3 0.1 fusion.39
  27.3 0.2 select_reduce_fusion.2
  27.5 0.1 pad_maximum_fusion.1
  27.6 0.1 copy.83
  27.7 3.9 copy.61
  31.7 0.5 broadcast_in_dim.28
  32.2 0.9 copy-done.2
  33.1 3.5 pad_maximum_fusion
  36.6 6.2 %copy.63 = bf16[136,16,640]{2,0,1:T(8,128)(2,1)} copy(bf16[136,16,640]{0,2,1:T(8,128)(2,1)} %pad_maximum_fusion) | data formatting | bytes 5570560 | tf_op jit(solution)/shard_map/concatenate | solution.py:72
  42.9 0.2 all-to-all-done.1
  43.0 7.0 %all-to-all-start = ((bf16[136,16,640]{2,0,1:T(8,128)(2,1)}), bf16[136,16,640]{2,0,1:T(8,128)(2,1)}, u32[]{:S(2)}, u32[]{:S(2)}) async-start(bf16[136,16,640]{2,0,1:T(8,128)(2,1)} %copy.63), calls=%async_computation | async-start | bytes 5570560 | tf_op jit(solution)/shard_map/all_to_all | solution.py:73
  50.1 0.0 all-gather.5.cloned.1.call-start
  50.1 1.5 fusion.25
  51.7 0.7 copy.90
  52.4 0.0 all-gather.5.cloned.1.call-update
  52.4 0.0 reduce-scatter.5.cloned.1.call-start
  52.4 52.1 %all-gather.5.cloned.1.call-done = bf16[1024,1024]{1,0:T(8,128)(2,1)} async-done(((bf16[64,1024]{1,0:T(8,128)(2,1)}), bf16[1024,1024]{1,0:T(8,128)(2,1)}) %all-gather.5.cloned.1.call-update) | async-done | bytes 2097168 | tf_op jit(solution)/shard_map/all_gather | solution.py:117
  104.5 8.7 %all-to-all-done = bf16[136,16,640]{2,0,1:T(8,128)(2,1)} async-done(((bf16[136,16,640]{2,0,1:T(8,128)(2,1)}), bf16[136,16,640]{2,0,1:T(8,128)(2,1)}, u32[]{:S(2)}, u32[]{:S(2)}) %all-to-all-start) | async-done | bytes 2785312 | tf_op jit(solution)/shard_map/all_to_all | solution.py:73
  113.2 4.2 fusion.65
  117.4 0.0 reduce-scatter.5.cloned.1.call-update
  117.5 0.0 reduce-scatter.7.cloned.1.call-start
  117.5 14.5 %reduce-scatter.5.cloned.1.call-done = f32[512,448]{0,1:T(8,128)} async-done(((f32[1024,448]{0,1:T(8,128)}), f32[512,448]{0,1:T(8,128)}) %reduce-scatter.5.cloned.1.call-update) | async-done | bytes 917520 | tf_op jit(solution)/shard_map/reduce_scatter | solution.py:120
  132.0 2.5 copy.80
  134.5 0.0 reduce-scatter.7.cloned.1.call-update
  134.5 0.0 all-gather.7.cloned.1.call-start
  134.6 39.8 %reduce-scatter.7.cloned.1.call-done = f32[64,448]{1,0:T(8,128)} async-done(((f32[512,448]{1,0:T(8,128)}), f32[64,448]{1,0:T(8,128)}) %reduce-scatter.7.cloned.1.call-update) | async-done | bytes 114704 | tf_op jit(solution)/shard_map/reduce_scatter | solution.py:121
  174.4 1.5 add_convert_fusion
  175.9 0.2 all-gather.9.cloned.1.call-start
  176.2 0.1 reshape.235
  176.2 0.8 slice_convert_fusion
  177.0 0.1 slice_compare_fusion
  177.1 0.1 fusion.63
  177.2 124.9 %all-gather.7.cloned.1.call-done = bf16[16384,448]{1,0:T(8,128)(2,1)} async-done(((bf16[64,448]{1,0:T(8,128)(2,1)}), bf16[16384,448]{1,0:T(8,128)(2,1)}) %all-gather.7.cloned.1.call-update) | async-done | bytes 14680080 | tf_op jit(solution)/shard_map/all_gather | solution.py:134
  302.0 11.9 %multiply_reduce_fusion = (f32[16,40]{1,0:T(8,128)S(1)}, f32[16,40,16,448]{3,1,2,0:T(8,128)}) fusion(bf16[16,16,64,448]{3,2,1,0:T(8,128)(2,1)} %bitcast.118, s32[16,40]{1,0:T(8,128)S(1)} %get-tuple-element.25, pred[16,40]{1,0:T(8,128)(4,1)S(1)} %slice_compare_fusion), kind=kOutput, calls=%fused_computation.1 | convolution fusion | flops 596458880 | bytes 33035904 | tf_op jit(solution)/shard_map/ncg,ndgk->ncdk/dot_general | solution.py:139
  314.0 13.5 %multiply_convert_fusion = bf16[16,40,16,448]{3,1,2,0:T(8,128)(2,1)} fusion(f32[16,40,16,448]{3,1,2,0:T(8,128)} %get-tuple-element.33, f32[16,448]{1,0:T(8,128)S(1)} %reshape.235, f32[16,40]{1,0:T(8,128)S(1)} %add_rsqrt_fusion), kind=kLoop, calls=%fused_computation | loop fusion | flops 13762560 | bytes 27556352 | tf_op jit(solution)/shard_map/convert_element_type | solution.py:147
  327.5 12.4 %copy.69 = bf16[16,40,16,448]{3,2,1,0:T(8,128)(2,1)} copy(bf16[16,40,16,448]{3,1,2,0:T(8,128)(2,1)} %multiply_convert_fusion) | data formatting | bytes 18350080 | tf_op jit(solution)/shard_map/convert_element_type | solution.py:147
  339.9 18.4 %convert_element_type.97 = bf16[640,7168]{1,0:T(8,128)(2,1)} reshape(bf16[16,40,16,448]{3,2,1,0:T(8,128)(2,1)} %copy.69) | data formatting | bytes 18350080 | tf_op jit(solution)/shard_map/convert_element_type | solution.py:147
  358.3 6.8 %fusion.10 = f32[640,128]{1,0:T(8,128)S(1)} fusion(bf16[640,7168]{1,0:T(8,128)(2,1)} %convert_element_type.97, bf16[1,7168,128]{2,1,0:T(8,128)(2,1)} %param.29), kind=kOutput, calls=%fused_computation.15 | convolution fusion | flops 1174405120 | bytes 11337728 | tf_op jit(solution)/shard_map/dot_general | solution.py:148
  365.0 0.4 copy-done.11
  365.5 3.2 fusion.21
  368.7 0.0 all-gather.9.cloned.1.call-update
  368.7 3.6 slice.56
  372.3 0.1 eq.83
  372.4 33.6 %all-gather.9.cloned.1.call-done = bf16[10240,128]{1,0:T(8,128)(2,1)} async-done(((bf16[640,128]{1,0:T(8,128)(2,1)}), bf16[10240,128]{1,0:T(8,128)(2,1)}) %all-gather.9.cloned.1.call-update) | async-done | bytes 2621456 | tf_op jit(solution)/shard_map/all_gather | solution.py:151
  406.0 4.4 copy.70
  410.4 3.4 fusion.29
  413.8 3.4 fusion.5
  417.3 1.7 fusion.16
  419.0 1.3 copy.73
  420.3 24.5 %all_to_all.46 = bf16[16,40,448]{2,1,0:T(8,128)(2,1)} all-to-all(bf16[16,40,448]{2,1,0:T(8,128)(2,1)S(1)} %bitcast.127), channel_id=1, replica_groups=mesh['role'=2,'dp'=16,'tensor'=8] {'role','tensor'}, dimensions={0} | all-to-all | bytes 1146880 | tf_op jit(solution)/shard_map/all_to_all | solution.py:167
  444.8 6.8 %all-to-all-start.3 = ((bf16[16,40,448]{2,1,0:T(8,128)(2,1)}), bf16[16,40,448]{2,1,0:T(8,128)(2,1)S(1)}, u32[]{:S(2)}, u32[]{:S(2)}) async-start(bf16[16,40,448]{2,1,0:T(8,128)(2,1)} %all_to_all.46), calls=%async_computation.4 | async-start | bytes 1310720 | tf_op jit(solution)/shard_map/all_to_all | solution.py:168
  451.7 12.1 %all-to-all-done.3 = bf16[16,40,448]{2,1,0:T(8,128)(2,1)S(1)} async-done(((bf16[16,40,448]{2,1,0:T(8,128)(2,1)}), bf16[16,40,448]{2,1,0:T(8,128)(2,1)S(1)}, u32[]{:S(2)}, u32[]{:S(2)}) %all-to-all-start.3) | async-done | bytes 573472 | tf_op jit(solution)/shard_map/all_to_all | solution.py:168
  463.8 1.1 fusion.26
  (42 shorter events, 0.3 us)
Async XLA Ops:
  6.5 410.7 %copy-start = (bf16[3,1,64,7168]{3,2,1,0:T(8,128)(2,1)S(1)}, bf16[3,1,64,7168]{3,2,1,0:T(8,128)(2,1)}, u32[]{:S(2)}) copy-start(bf16[3,1,64,7168]{3,2,1,0:T(8,128)(2,1)} %param.33) | copy-start | bytes 8257540
  8.9 6.1 %slice-start = ((s8[4718592]{0:T(1024)(128)(4,1)}), s8[4194304]{0:T(1024)(128)(4,1)S(1)}, s32[]{:S(2)}) async-start(s8[4718592]{0:T(1024)(128)(4,1)} %bitcast.120), calls=%async_computation.11 | async-start | bytes 8388608
  10.5 4.4 slice-start.1
  16.8 10.2 %copy-start.7 = (s32[64,8]{0,1:T(8,128)S(1)}, s32[64,8]{0,1:T(8,128)}, u32[]{:S(2)}) copy-start(s32[64,8]{0,1:T(8,128)} %param.26) | copy-start | bytes 6148
  16.8 10.6 %copy-start.10 = (s32[64]{0:T(128)S(1)}, s32[64]{0:T(128)}, u32[]{:S(2)}) copy-start(s32[64]{0:T(128)} %param.28) | copy-start | bytes 772
  18.3 13.4 %copy-start.6 = (bf16[3,1,128,64]{2,3,1,0:T(8,128)(2,1)S(1)}, bf16[3,1,128,64]{2,3,1,0:T(8,128)(2,1)}, u32[]{:S(2)}) copy-start(bf16[3,1,128,64]{2,3,1,0:T(8,128)(2,1)} %param.32) | copy-start | bytes 147460
  18.3 24.8 %all-to-all-start.1 = ((bf16[8,64,512]{2,0,1:T(8,128)(2,1)}), bf16[8,64,512]{2,0,1:T(8,128)(2,1)S(1)}, u32[]{:S(2)}, u32[]{:S(2)}) async-start(bf16[8,64,512]{2,0,1:T(8,128)(2,1)} %copy.65), calls=%async_computation.1 | async-start | bytes 1048576 | tf_op jit(solution)/shard_map/all_to_all | solution.py:110
  31.6 1.5 copy-start.2
  43.0 70.2 %all-to-all-start = ((bf16[136,16,640]{2,0,1:T(8,128)(2,1)}), bf16[136,16,640]{2,0,1:T(8,128)(2,1)}, u32[]{:S(2)}, u32[]{:S(2)}) async-start(bf16[136,16,640]{2,0,1:T(8,128)(2,1)} %copy.63), calls=%async_computation | async-start | bytes 5570560 | tf_op jit(solution)/shard_map/all_to_all | solution.py:73
  50.1 54.4 %all-gather.5.cloned.1.call-start = ((), (), s32[]{:S(2)}) async-start(), calls=%async_computation.6 | async-start | bytes 2228224 | tf_op jit(solution)/shard_map/all_gather | solution.py:117
  52.4 79.7 %reduce-scatter.5.cloned.1.call-start = ((), (), s32[]{:S(2)}) async-start(), calls=%async_computation.7 | async-start | bytes 2752512 | tf_op jit(solution)/shard_map/reduce_scatter | solution.py:120
  117.4 56.9 %copy-start.5 = (bf16[64,448]{1,0:T(8,128)(2,1)S(1)}, bf16[64,448]{1,0:T(8,128)(2,1)}, u32[]{:S(2)}) copy-start(bf16[64,448]{1,0:T(8,128)(2,1)} %param.24) | copy-start | bytes 172036
  117.4 58.7 %copy-start.8 = (bf16[7168]{0:T(1024)(128)(2,1)S(1)}, bf16[7168]{0:T(1024)(128)(2,1)}, u32[]{:S(2)}) copy-start(bf16[7168]{0:T(1024)(128)(2,1)} %param.25) | copy-start | bytes 43012
  117.5 56.9 %reduce-scatter.7.cloned.1.call-start = ((), (), s32[]{:S(2)}) async-start(), calls=%async_computation.10 | async-start | bytes 1179648 | tf_op jit(solution)/shard_map/reduce_scatter | solution.py:121
  134.5 167.5 %all-gather.7.cloned.1.call-start = ((), (), s32[]{:S(2)}) async-start(), calls=%async_computation.8 | async-start | bytes 16842752 | tf_op jit(solution)/shard_map/all_gather | solution.py:134
  175.9 230.1 %all-gather.9.cloned.1.call-start = ((), (), s32[]{:S(2)}) async-start(), calls=%async_computation.9 | async-start | bytes 2785280 | tf_op jit(solution)/shard_map/all_gather | solution.py:151
  358.3 6.8 %copy-start.1 = (bf16[640,7168]{1,0:T(8,128)(2,1)S(1)}, bf16[640,7168]{1,0:T(8,128)(2,1)}, u32[]{:S(2)}) copy-start(bf16[640,7168]{1,0:T(8,128)(2,1)} %convert_element_type.97) | copy-start | bytes 27525124
  358.3 7.2 %copy-start.11 = (bf16[1,7168,128]{2,1,0:T(8,128)(2,1)S(1)}, bf16[1,7168,128]{2,1,0:T(8,128)(2,1)}, u32[]{:S(2)}) copy-start(bf16[1,7168,128]{2,1,0:T(8,128)(2,1)} %param.30) | copy-start | bytes 5505028
  410.4 3.4 copy-start.3
  417.2 34.4 %copy-start.9 = (f32[64,8]{0,1:T(8,128)S(1)}, f32[64,8]{0,1:T(8,128)}, u32[]{:S(2)}) copy-start(f32[64,8]{0,1:T(8,128)} %param.27) | copy-start | bytes 6148
  417.2 46.6 %copy-start.4 = (bf16[64,448]{1,0:T(8,128)(2,1)S(1)}, bf16[64,448]{1,0:T(8,128)(2,1)}, u32[]{:S(2)}) copy-start(bf16[64,448]{1,0:T(8,128)(2,1)} %add_convert_fusion) | copy-start | bytes 172036
  444.8 19.0 %all-to-all-start.3 = ((bf16[16,40,448]{2,1,0:T(8,128)(2,1)}), bf16[16,40,448]{2,1,0:T(8,128)(2,1)S(1)}, u32[]{:S(2)}, u32[]{:S(2)}) async-start(bf16[16,40,448]{2,1,0:T(8,128)(2,1)} %all_to_all.46), calls=%async_computation.4 | async-start | bytes 1310720 | tf_op jit(solution)/shard_map/all_to_all | solution.py:168
Sparse Core Ops, SparseCore 0:
  53.3 51.1 all-gather.4
  117.6 14.4 reduce-scatter.4
  134.7 39.6 reduce-scatter.6
  177.8 124.1 all-gather.6
  368.8 37.1 all-gather.8
where the time goes:
time: 473 us; the launch traced here: 471 us
  waiting for transfers between devices  286 us (60%)
  local copies, waits for them, and re-layouts  58.4 us (12%)
  matrix products  44.8 us (9%)
  blocking collectives  24.5 us (5%)
  starting transfers between devices  22.9 us (5%)
  other arithmetic  21.3 us (5%)
  between operations  13.4 us (3%)
    all_gather x1, waiting for transfers between devices, local(): lax.all_gather(mixed_in, ('role', 'tensor', 'dp'), axis=0, tiled=True)  125 us
    all_gather x1, waiting for transfers between devices, local(): all_values = lax.all_gather(head_values, 'dp', axis=0, tiled=True)  52.1 us
    reduce_scatter x1, waiting for transfers between devices, local(): lax.psum_scatter(partial, 'tensor', scatter_dimension=0, tiled=True)  39.8 us
    all_gather x1, waiting for transfers between devices, local(): gathered = lax.all_gather(hidden, RT, axis=0, tiled=False)  33.6 us
    convert_element_type x2, local copies, waits for them, and re-layouts, local(): (picked * scale * norm_gain.astype(jnp.float32)).astype(jnp.bfloat16)  30.8 us
    all_to_all x1, blocking collectives, local(): lax.all_to_all(expert_out, RT, split_axis=0, concat_axis=0, tiled=True)  24.5 us
    reduce_scatter x1, waiting for transfers between devices, local(): partial = lax.psum_scatter(partial, 'role', scatter_dimension=0, tiled=True)  14.5 us
    convert_element_type x1, other arithmetic, local(): (picked * scale * norm_gain.astype(jnp.float32)).astype(jnp.bfloat16)  13.5 us
  transfers between devices with their start and end apart: 8, of which 8 were waited for; matrix products, arithmetic and copies ran while one was open for 5% of the time, Pallas kernels for 0%

commit v1 on v0

--- a/solution.py
+++ b/solution.py
@@ -10,6 +10,34 @@
 NORM_EPS = 1e-06
 MASKED = -1e30
 RT = ("role", "tensor")
+
+
+def tell_marks(target, dim_at):
+    target = jnp.moveaxis(target, 0, dim_at)
+    y2 = target.shape
+    return target.reshape(*y2[:dim_at], y2[dim_at] * y2[dim_at + 1], *y2[dim_at + 2 :])
+
+
+def clear_the_sums_all(sample, axis_tag, dim_k):
+    parts_n = lax.axis_size(axis_tag)
+    frames = tuple(((dev_j, (dev_j + 1) % parts_n) for dev_j in range(parts_n)))
+    prior, reply = ([], [])
+    series = tuple(((tick, j0) for j0, tick in frames))
+    pp = 0
+    while pp < parts_n - 1:
+        if pp % 2 == 0:
+            prior.append(
+                lax.ppermute(prior[-1] if prior else sample, axis_name=axis_tag, perm=frames)
+            )
+        else:
+            reply.append(
+                lax.ppermute(reply[-1] if reply else sample, axis_name=axis_tag, perm=series)
+            )
+        pp += 1
+    block_next = jnp.stack([*prior[::-1], sample, *reply], axis=0)
+    mid_arr = lax.axis_index(axis_tag) - len(prior)
+    block_next = block_next[(jnp.arange(parts_n) - mid_arr) % parts_n]
+    return tell_marks(block_next, dim_k)
 
 
 def rms_rows(input_rows, norm_gain):
@@ -114,7 +142,7 @@
     head_values = head_values.reshape(
         head_values.shape[0], head_values.shape[1] * head_values.shape[2]
     )
-    all_values = lax.all_gather(head_values, "dp", axis=0, tiled=True)
+    all_values = clear_the_sums_all(head_values, "dp", 0)
     down_pack, all_values = lax.optimization_barrier((down_pack, all_values))
     partial = jnp.dot(all_values, out_proj, preferred_element_type=jnp.float32)
     partial = lax.psum_scatter(partial, "role", scatter_dimension=0, tiled=True)

time: 473 us -> 507 us (1.072); the launches traced: 471 us -> 497 us
  starting transfers between devices: 22.9 us -> 62.4 us
  waiting for transfers between devices: 286 us -> 249 us
  local copies, waits for them, and re-layouts: 58.4 us -> 81.2 us
    all_gather x1 -> x0, waiting for transfers between devices: 52.1 us -> none  [local(): all_values = lax.all_gather(head_values, 'dp', axis=0, tiled=True)]
    ppermute x0 -> x15, starting transfers between devices: none -> 39.5 us  [the longest x7 37.4 us: clear_the_sums_all(): lax.ppermute(reply[-1] if reply else sample, axis_name=axis_tag, perm=ser...]
    ppermute x0 -> x15, waiting for transfers between devices: none -> 26.5 us  [the longest x8 26.5 us: clear_the_sums_all(): lax.ppermute(prior[-1] if prior else sample, axis_name=axis_tag, perm=fra...]
    unnamed x31 -> x64, local copies, waits for them, and re-layouts: 7.95 us -> 26.5 us
    all_to_all x1, waiting for transfers between devices: 8.75 us -> 0.01 us  [local(): lax.all_to_all(down_pack, RT, split_axis=1, concat_axis=0, tiled=True)]
  transfers between devices with their start and end apart: 8 -> 22, of which waited for: 8 -> 14; matrix products, arithmetic and copies ran while one was open for 5% -> 9% of each run, Pallas kernels for 0% -> 0%
where the time goes in v1:
time: 507 us; the launch traced here: 497 us
  waiting for transfers between devices  249 us (49%)
  local copies, waits for them, and re-layouts  81.2 us (16%)
  starting transfers between devices  62.4 us (12%)
  matrix products  44.9 us (9%)
  blocking collectives  24.5 us (5%)
  other arithmetic  22 us (4%)
  between operations  13.8 us (3%)
    all_gather x1, waiting for transfers between devices, local(): lax.all_gather(mixed_in, ('role', 'tensor', 'dp'), axis=0, tiled=True)  125 us
    reduce_scatter x1, waiting for transfers between devices, local(): lax.psum_scatter(partial, 'tensor', scatter_dimension=0, tiled=True)  39.8 us
    ppermute x7, starting transfers between devices, clear_the_sums_all(): lax.ppermute(reply[-1] if reply else sample, axis_name=axis_tag, perm=ser...  37.4 us
    all_gather x1, waiting for transfers between devices, local(): gathered = lax.all_gather(hidden, RT, axis=0, tiled=False)  33.5 us
    convert_element_type x2, local copies, waits for them, and re-layouts, local(): (picked * scale * norm_gain.astype(jnp.float32)).astype(jnp.bfloat16)  30.8 us
    ppermute x8, waiting for transfers between devices, clear_the_sums_all(): lax.ppermute(prior[-1] if prior else sample, axis_name=axis_tag, perm=fra...  26.5 us
    unnamed x64, local copies, waits for them, and re-layouts  26.5 us
    all_to_all x1, blocking collectives, local(): lax.all_to_all(expert_out, RT, split_axis=0, concat_axis=0, tiled=True)  24.5 us
  transfers between devices with their start and end apart: 22, of which 14 were waited for; matrix products, arithmetic and copies ran while one was open for 9% of the time, Pallas kernels for 0%

profile of v1, /device:TPU:32, one launch (start us, length us, event | category | flops | bytes accessed | tf_op | source)
XLA Modules:
  0.0 497.4 jit_solution(2604167252119899325)
XLA Ops:
  6.5 0.9 reshape.299
  7.4 0.7 reshape.277
  8.1 0.7 iota_compare_fusion.4
  8.9 1.7 fusion.65
  10.5 3.8 fusion.7
  15.0 1.7 fusion.2
  17.1 1.1 copy.67
  18.3 8.6 %all-to-all-start.1 = ((bf16[8,64,512]{2,0,1:T(8,128)(2,1)}), bf16[8,64,512]{2,0,1:T(8,128)(2,1)S(1)}, u32[]{:S(2)}, u32[]{:S(2)}) async-start(bf16[8,64,512]{2,0,1:T(8,128)(2,1)} %copy.67), calls=%async_computation.1 | async-start | bytes 1048576 | tf_op jit(solution)/shard_map/all_to_all | solution.py:138
  27.6 3.9 copy.63
  32.1 0.9 copy-done.2
  33.0 3.5 pad_maximum_fusion
  36.5 6.3 %copy.65 = bf16[136,16,640]{2,0,1:T(8,128)(2,1)} copy(bf16[136,16,640]{0,2,1:T(8,128)(2,1)} %pad_maximum_fusion) | data formatting | bytes 5570560 | tf_op jit(solution)/shard_map/concatenate | solution.py:100
  42.9 7.1 %all-to-all-start = ((bf16[136,16,640]{2,0,1:T(8,128)(2,1)}), bf16[136,16,640]{2,0,1:T(8,128)(2,1)}, u32[]{:S(2)}, u32[]{:S(2)}) async-start(bf16[136,16,640]{2,0,1:T(8,128)(2,1)} %copy.65), calls=%async_computation | async-start | bytes 5570560 | tf_op jit(solution)/shard_map/all_to_all | solution.py:101
  50.1 1.5 convolution_convert_fusion
  51.6 1.7 collective-permute-start
  53.3 7.4 %collective-permute-done = bf16[64,1024]{1,0:T(8,128)(2,1)S(1)} collective-permute-done((bf16[64,1024]{1,0:T(8,128)(2,1)S(1)}, bf16[64,1024]{1,0:T(8,128)(2,1)S(1)}, u32[]{:S(2)}, u32[]{:S(2)}) %collective-permute-start) | collective-permute-done | bytes 131104 | tf_op jit(solution)/shard_map/ppermute | solution.py:30
  60.7 5.3 %collective-permute-start.8 = (bf16[64,1024]{1,0:T(8,128)(2,1)S(1)}, bf16[64,1024]{1,0:T(8,128)(2,1)S(1)}, u32[]{:S(2)}, u32[]{:S(2)}) collective-permute-start(bf16[64,1024]{1,0:T(8,128)(2,1)S(1)} %copy_bitcast_fusion), channel_id=1, source_target_pairs={{8,0},{16,8},{24,16},{32,24},{40,32},{48,40},{56,48},{64,56},{72,6... | collective-permute-start | bytes 393224 | tf_op jit(solution)/shard_map/ppermute | solution.py:34
  66.1 2.9 collective-permute-done.1
  69.0 5.3 %collective-permute-start.9 = (bf16[64,1024]{1,0:T(8,128)(2,1)S(1)}, bf16[64,1024]{1,0:T(8,128)(2,1)S(1)}, u32[]{:S(2)}, u32[]{:S(2)}) collective-permute-start(bf16[64,1024]{1,0:T(8,128)(2,1)S(1)} %collective-permute-done.8), channel_id=1, source_target_pairs={{8,0},{16,8},{24,16},{32,24},{40,32},{48,40},{56,48},{64,56},{72,6... | collective-permute-start | bytes 393224 | tf_op jit(solution)/shard_map/ppermute | solution.py:34
  74.3 2.9 collective-permute-done.2
  77.3 0.7 copy-done.5
  78.0 5.3 %collective-permute-start.10 = (bf16[64,1024]{1,0:T(8,128)(2,1)S(1)}, bf16[64,1024]{1,0:T(8,128)(2,1)S(1)}, u32[]{:S(2)}, u32[]{:S(2)}) collective-permute-start(bf16[64,1024]{1,0:T(8,128)(2,1)S(1)} %collective-permute-done.9), channel_id=1, source_target_pairs={{8,0},{16,8},{24,16},{32,24},{40,32},{48,40},{56,48},{64,56},{72,6... | collective-permute-start | bytes 393224 | tf_op jit(solution)/shard_map/ppermute | solution.py:34
  83.3 2.3 collective-permute-done.3
  86.1 5.5 %collective-permute-start.11 = (bf16[64,1024]{1,0:T(8,128)(2,1)S(1)}, bf16[64,1024]{1,0:T(8,128)(2,1)S(1)}, u32[]{:S(2)}, u32[]{:S(2)}) collective-permute-start(bf16[64,1024]{1,0:T(8,128)(2,1)S(1)} %collective-permute-done.10), channel_id=1, source_target_pairs={{8,0},{16,8},{24,16},{32,24},{40,32},{48,40},{56,48},{64,56},{72,6... | collective-permute-start | bytes 393224 | tf_op jit(solution)/shard_map/ppermute | solution.py:34
  91.6 2.7 collective-permute-done.4
  95.0 4.9 collective-permute-start.12
  99.9 2.8 collective-permute-done.5
  102.7 5.6 %collective-permute-start.13 = (bf16[64,1024]{1,0:T(8,128)(2,1)}, bf16[64,1024]{1,0:T(8,128)(2,1)}, u32[]{:S(2)}, u32[]{:S(2)}) collective-permute-start(bf16[64,1024]{1,0:T(8,128)(2,1)} %collective-permute-done.12), channel_id=1, source_target_pairs={{8,0},{16,8},{24,16},{32,24},{40,32},{48,40},{56,48},{64,56},{72,6... | collective-permute-start | bytes 393224 | tf_op jit(solution)/shard_map/ppermute | solution.py:34
  108.3 3.0 collective-permute-done.6
  112.1 5.4 %collective-permute-start.14 = (bf16[64,1024]{1,0:T(8,128)(2,1)}, bf16[64,1024]{1,0:T(8,128)(2,1)S(1)}, u32[]{:S(2)}, u32[]{:S(2)}) collective-permute-start(bf16[64,1024]{1,0:T(8,128)(2,1)} %collective-permute-done.13), channel_id=1, source_target_pairs={{8,0},{16,8},{24,16},{32,24},{40,32},{48,40},{56,48},{64,56},{72,6... | collective-permute-start | bytes 393224 | tf_op jit(solution)/shard_map/ppermute | solution.py:34
  117.6 2.4 collective-permute-done.7
  119.9 1.6 bitcast_dynamic-update-slice_fusion.14
  121.5 1.6 bitcast_dynamic-update-slice_fusion.13
  123.0 1.6 bitcast_dynamic-update-slice_fusion.12
  124.6 1.6 bitcast_dynamic-update-slice_fusion.11
  126.2 1.6 bitcast_dynamic-update-slice_fusion.10
  127.7 1.6 bitcast_dynamic-update-slice_fusion.9
  133.9 1.6 bitcast_dynamic-update-slice_fusion.2
  135.5 1.6 bitcast_dynamic-update-slice_fusion.1
  137.7 3.7 gather_fusion
  141.4 4.2 fusion.66
  145.7 11.5 %reduce-scatter.5.cloned.1.call-done = f32[512,448]{0,1:T(8,128)} async-done(((f32[1024,448]{0,1:T(8,128)}), f32[512,448]{0,1:T(8,128)}) %reduce-scatter.5.cloned.1.call-update) | async-done | bytes 917520 | tf_op jit(solution)/shard_map/reduce_scatter | solution.py:148
  157.2 2.5 copy.83
  159.8 39.8 %reduce-scatter.7.cloned.1.call-done = f32[64,448]{1,0:T(8,128)} async-done(((f32[512,448]{1,0:T(8,128)}), f32[64,448]{1,0:T(8,128)}) %reduce-scatter.7.cloned.1.call-update) | async-done | bytes 114704 | tf_op jit(solution)/shard_map/reduce_scatter | solution.py:149
  199.6 1.5 add_convert_fusion
  201.5 0.8 slice_convert_fusion
  202.4 125.0 %all-gather.4.cloned.1.call-done = bf16[16384,448]{1,0:T(8,128)(2,1)} async-done(((bf16[64,448]{1,0:T(8,128)(2,1)}), bf16[16384,448]{1,0:T(8,128)(2,1)}) %all-gather.4.cloned.1.call-update) | async-done | bytes 14680080 | tf_op jit(solution)/shard_map/all_gather | solution.py:162
  327.4 12.0 %multiply_reduce_fusion = (f32[16,40]{1,0:T(8,128)S(1)}, f32[16,40,16,448]{3,1,2,0:T(8,128)}) fusion(bf16[16,16,64,448]{3,2,1,0:T(8,128)(2,1)} %bitcast.151, s32[16,40]{1,0:T(8,128)S(1)} %get-tuple-element.25, pred[16,40]{1,0:T(8,128)(4,1)S(1)} %slice_compare_fusion), kind=kOutput, calls=%fused_computation.2 | convolution fusion | flops 596458880 | bytes 33035904 | tf_op jit(solution)/shard_map/ncg,ndgk->ncdk/dot_general | solution.py:167
  339.4 13.5 %multiply_convert_fusion = bf16[16,40,16,448]{3,1,2,0:T(8,128)(2,1)} fusion(f32[16,40,16,448]{3,1,2,0:T(8,128)} %get-tuple-element.33, f32[16,448]{1,0:T(8,128)S(1)} %reshape.288, f32[16,40]{1,0:T(8,128)S(1)} %add_rsqrt_fusion), kind=kLoop, calls=%fused_computation.1 | loop fusion | flops 13762560 | bytes 27556352 | tf_op jit(solution)/shard_map/convert_element_type | solution.py:175
  352.9 12.4 %copy.72 = bf16[16,40,16,448]{3,2,1,0:T(8,128)(2,1)} copy(bf16[16,40,16,448]{3,1,2,0:T(8,128)(2,1)} %multiply_convert_fusion) | data formatting | bytes 18350080 | tf_op jit(solution)/shard_map/convert_element_type | solution.py:175
  365.4 18.4 %convert_element_type.97 = bf16[640,7168]{1,0:T(8,128)(2,1)} reshape(bf16[16,40,16,448]{3,2,1,0:T(8,128)(2,1)} %copy.72) | data formatting | bytes 18350080 | tf_op jit(solution)/shard_map/convert_element_type | solution.py:175
  383.8 6.8 %fusion.10 = f32[640,128]{1,0:T(8,128)S(1)} fusion(bf16[640,7168]{1,0:T(8,128)(2,1)} %convert_element_type.97, bf16[1,7168,128]{2,1,0:T(8,128)(2,1)} %param.29), kind=kOutput, calls=%fused_computation.16 | convolution fusion | flops 1174405120 | bytes 11337728 | tf_op jit(solution)/shard_map/dot_general | solution.py:176
  391.0 3.2 fusion.21
  394.2 3.6 slice.58
  398.0 33.5 %all-gather.6.cloned.1.call-done = bf16[10240,128]{1,0:T(8,128)(2,1)} async-done(((bf16[640,128]{1,0:T(8,128)(2,1)}), bf16[10240,128]{1,0:T(8,128)(2,1)}) %all-gather.6.cloned.1.call-update) | async-done | bytes 2621456 | tf_op jit(solution)/shard_map/all_gather | solution.py:179
  431.5 4.6 copy.73
  436.1 3.4 fusion.28
  439.5 3.4 fusion.5
  442.9 1.7 fusion.16
  444.7 1.3 copy.76
  446.0 24.5 %all_to_all.46 = bf16[16,40,448]{2,1,0:T(8,128)(2,1)} all-to-all(bf16[16,40,448]{2,1,0:T(8,128)(2,1)S(1)} %bitcast.160), channel_id=1, replica_groups=mesh['role'=2,'dp'=16,'tensor'=8] {'role','tensor'}, dimensions={0} | all-to-all | bytes 1146880 | tf_op jit(solution)/shard_map/all_to_all | solution.py:195
  470.5 6.8 %all-to-all-start.3 = ((bf16[16,40,448]{2,1,0:T(8,128)(2,1)}), bf16[16,40,448]{2,1,0:T(8,128)(2,1)S(1)}, u32[]{:S(2)}, u32[]{:S(2)}) async-start(bf16[16,40,448]{2,1,0:T(8,128)(2,1)} %all_to_all.46), calls=%async_computation.4 | async-start | bytes 1310720 | tf_op jit(solution)/shard_map/all_to_all | solution.py:196
  477.4 12.1 %all-to-all-done.3 = bf16[16,40,448]{2,1,0:T(8,128)(2,1)S(1)} async-done(((bf16[16,40,448]{2,1,0:T(8,128)(2,1)}), bf16[16,40,448]{2,1,0:T(8,128)(2,1)S(1)}, u32[]{:S(2)}, u32[]{:S(2)}) %all-to-all-start.3) | async-done | bytes 573472 | tf_op jit(solution)/shard_map/all_to_all | solution.py:196
  489.5 1.1 fusion.25
  (108 shorter events, 10.9 us)
Async XLA Ops:
  6.5 436.4 %copy-start = (bf16[3,1,64,7168]{3,2,1,0:T(8,128)(2,1)S(1)}, bf16[3,1,64,7168]{3,2,1,0:T(8,128)(2,1)}, u32[]{:S(2)}) copy-start(bf16[3,1,64,7168]{3,2,1,0:T(8,128)(2,1)} %param.33) | copy-start | bytes 8257540
  8.9 6.1 %slice-start = ((s8[4718592]{0:T(1024)(128)(4,1)}), s8[4194304]{0:T(1024)(128)(4,1)S(1)}, s32[]{:S(2)}) async-start(s8[4718592]{0:T(1024)(128)(4,1)} %bitcast.153), calls=%async_computation.10 | async-start | bytes 8388608
  10.5 4.4 slice-start.1
  16.8 10.1 %copy-start.16 = (s32[64,8]{0,1:T(8,128)S(1)}, s32[64,8]{0,1:T(8,128)}, u32[]{:S(2)}) copy-start(s32[64,8]{0,1:T(8,128)} %param.26) | copy-start | bytes 6148
  17.1 10.1 %copy-start.19 = (s32[64]{0:T(128)S(1)}, s32[64]{0:T(128)}, u32[]{:S(2)}) copy-start(s32[64]{0:T(128)} %param.28) | copy-start | bytes 772
  18.3 24.6 %all-to-all-start.1 = ((bf16[8,64,512]{2,0,1:T(8,128)(2,1)}), bf16[8,64,512]{2,0,1:T(8,128)(2,1)S(1)}, u32[]{:S(2)}, u32[]{:S(2)}) async-start(bf16[8,64,512]{2,0,1:T(8,128)(2,1)} %copy.67), calls=%async_computation.1 | async-start | bytes 1048576 | tf_op jit(solution)/shard_map/all_to_all | solution.py:138
  26.9 4.7 copy-start.15
  31.5 1.5 copy-start.2
  42.9 98.5 %all-to-all-start = ((bf16[136,16,640]{2,0,1:T(8,128)(2,1)}), bf16[136,16,640]{2,0,1:T(8,128)(2,1)}, u32[]{:S(2)}, u32[]{:S(2)}) async-start(bf16[136,16,640]{2,0,1:T(8,128)(2,1)} %copy.65), calls=%async_computation | async-start | bytes 5570560 | tf_op jit(solution)/shard_map/all_to_all | solution.py:101
  50.0 107.2 %reduce-scatter.5.cloned.1.call-start = ((), (), s32[]{:S(2)}) async-start(), calls=%async_computation.6 | async-start | bytes 2752512 | tf_op jit(solution)/shard_map/reduce_scatter | solution.py:148
  51.6 9.1 %collective-permute-start = (bf16[64,1024]{1,0:T(8,128)(2,1)S(1)}, bf16[64,1024]{1,0:T(8,128)(2,1)S(1)}, u32[]{:S(2)}, u32[]{:S(2)}) collective-permute-start(bf16[64,1024]{1,0:T(8,128)(2,1)S(1)} %copy_bitcast_fusion), channel_id=1, source_target_pairs={{0,8},{8,16},{16,24},{24,32},{32,40},{40,48},{48,56},{56,64},{64,7... | collective-permute-start | bytes 393224 | tf_op jit(solution)/shard_map/ppermute | solution.py:30
  60.7 8.3 %collective-permute-start.1 = (bf16[64,1024]{1,0:T(8,128)(2,1)S(1)}, bf16[64,1024]{1,0:T(8,128)(2,1)S(1)}, u32[]{:S(2)}, u32[]{:S(2)}) collective-permute-start(bf16[64,1024]{1,0:T(8,128)(2,1)S(1)} %collective-permute-done), channel_id=1, source_target_pairs={{0,8},{8,16},{16,24},{24,32},{32,40},{40,48},{48,56},{56,64},{64,7... | collective-permute-start | bytes 393224 | tf_op jit(solution)/shard_map/ppermute | solution.py:30
  60.7 8.3 %collective-permute-start.8 = (bf16[64,1024]{1,0:T(8,128)(2,1)S(1)}, bf16[64,1024]{1,0:T(8,128)(2,1)S(1)}, u32[]{:S(2)}, u32[]{:S(2)}) collective-permute-start(bf16[64,1024]{1,0:T(8,128)(2,1)S(1)} %copy_bitcast_fusion), channel_id=1, source_target_pairs={{8,0},{16,8},{24,16},{32,24},{40,32},{48,40},{56,48},{64,56},{72,6... | collective-permute-start | bytes 393224 | tf_op jit(solution)/shard_map/ppermute | solution.py:34
  69.0 8.3 %collective-permute-start.2 = (bf16[64,1024]{1,0:T(8,128)(2,1)S(1)}, bf16[64,1024]{1,0:T(8,128)(2,1)S(1)}, u32[]{:S(2)}, u32[]{:S(2)}) collective-permute-start(bf16[64,1024]{1,0:T(8,128)(2,1)S(1)} %collective-permute-done.1), channel_id=1, source_target_pairs={{0,8},{8,16},{16,24},{24,32},{32,40},{40,48},{48,56},{56,64},{64,7... | collective-permute-start | bytes 393224 | tf_op jit(solution)/shard_map/ppermute | solution.py:30
  69.0 8.3 %collective-permute-start.9 = (bf16[64,1024]{1,0:T(8,128)(2,1)S(1)}, bf16[64,1024]{1,0:T(8,128)(2,1)S(1)}, u32[]{:S(2)}, u32[]{:S(2)}) collective-permute-start(bf16[64,1024]{1,0:T(8,128)(2,1)S(1)} %collective-permute-done.8), channel_id=1, source_target_pairs={{8,0},{16,8},{24,16},{32,24},{40,32},{48,40},{56,48},{64,56},{72,6... | collective-permute-start | bytes 393224 | tf_op jit(solution)/shard_map/ppermute | solution.py:34
  77.3 8.8 %copy-start.7 = (bf16[64,1024]{1,0:T(8,128)(2,1)}, bf16[64,1024]{1,0:T(8,128)(2,1)S(1)}, u32[]{:S(2)}) copy-start(bf16[64,1024]{1,0:T(8,128)(2,1)S(1)} %collective-permute-done.2) | copy-start | bytes 393220
  77.3 8.3 %collective-permute-start.3 = (bf16[64,1024]{1,0:T(8,128)(2,1)S(1)}, bf16[64,1024]{1,0:T(8,128)(2,1)S(1)}, u32[]{:S(2)}, u32[]{:S(2)}) collective-permute-start(bf16[64,1024]{1,0:T(8,128)(2,1)S(1)} %collective-permute-done.2), channel_id=1, source_target_pairs={{0,8},{8,16},{16,24},{24,32},{32,40},{40,48},{48,56},{56,64},{64,7... | collective-permute-start | bytes 393224 | tf_op jit(solution)/shard_map/ppermute | solution.py:30
  77.3 0.7 copy-start.5
  78.0 8.0 %collective-permute-start.10 = (bf16[64,1024]{1,0:T(8,128)(2,1)S(1)}, bf16[64,1024]{1,0:T(8,128)(2,1)S(1)}, u32[]{:S(2)}, u32[]{:S(2)}) collective-permute-start(bf16[64,1024]{1,0:T(8,128)(2,1)S(1)} %collective-permute-done.9), channel_id=1, source_target_pairs={{8,0},{16,8},{24,16},{32,24},{40,32},{48,40},{56,48},{64,56},{72,6... | collective-permute-start | bytes 393224 | tf_op jit(solution)/shard_map/ppermute | solution.py:34
  85.6 26.4 %copy-start.12 = (bf16[64,1024]{1,0:T(8,128)(2,1)}, bf16[64,1024]{1,0:T(8,128)(2,1)S(1)}, u32[]{:S(2)}) copy-start(bf16[64,1024]{1,0:T(8,128)(2,1)S(1)} %collective-permute-done.3) | copy-start | bytes 393220
  85.6 8.7 %collective-permute-start.4 = (bf16[64,1024]{1,0:T(8,128)(2,1)S(1)}, bf16[64,1024]{1,0:T(8,128)(2,1)S(1)}, u32[]{:S(2)}, u32[]{:S(2)}) collective-permute-start(bf16[64,1024]{1,0:T(8,128)(2,1)S(1)} %collective-permute-done.3), channel_id=1, source_target_pairs={{0,8},{8,16},{16,24},{24,32},{32,40},{40,48},{48,56},{56,64},{64,7... | collective-permute-start | bytes 393224 | tf_op jit(solution)/shard_map/ppermute | solution.py:30
  86.1 5.5 %copy-start.8 = (bf16[64,1024]{1,0:T(8,128)(2,1)}, bf16[64,1024]{1,0:T(8,128)(2,1)S(1)}, u32[]{:S(2)}) copy-start(bf16[64,1024]{1,0:T(8,128)(2,1)S(1)} %collective-permute-done.10) | copy-start | bytes 393220
  86.1 8.3 %collective-permute-start.11 = (bf16[64,1024]{1,0:T(8,128)(2,1)S(1)}, bf16[64,1024]{1,0:T(8,128)(2,1)S(1)}, u32[]{:S(2)}, u32[]{:S(2)}) collective-permute-start(bf16[64,1024]{1,0:T(8,128)(2,1)S(1)} %collective-permute-done.10), channel_id=1, source_target_pairs={{8,0},{16,8},{24,16},{32,24},{40,32},{48,40},{56,48},{64,56},{72,6... | collective-permute-start | bytes 393224 | tf_op jit(solution)/shard_map/ppermute | solution.py:34
  94.3 0.7 copy-start.13
  94.3 8.4 %collective-permute-start.5 = (bf16[64,1024]{1,0:T(8,128)(2,1)S(1)}, bf16[64,1024]{1,0:T(8,128)(2,1)}, u32[]{:S(2)}, u32[]{:S(2)}) collective-permute-start(bf16[64,1024]{1,0:T(8,128)(2,1)S(1)} %collective-permute-done.4), channel_id=1, source_target_pairs={{0,8},{8,16},{16,24},{24,32},{32,40},{40,48},{48,56},{56,64},{64,7... | collective-permute-start | bytes 393224 | tf_op jit(solution)/shard_map/ppermute | solution.py:30
  95.0 17.0 %copy-start.10 = (bf16[64,1024]{1,0:T(8,128)(2,1)}, bf16[64,1024]{1,0:T(8,128)(2,1)S(1)}, u32[]{:S(2)}) copy-start(bf16[64,1024]{1,0:T(8,128)(2,1)S(1)} %collective-permute-done.11) | copy-start | bytes 393220
  95.0 7.7 %collective-permute-start.12 = (bf16[64,1024]{1,0:T(8,128)(2,1)S(1)}, bf16[64,1024]{1,0:T(8,128)(2,1)}, u32[]{:S(2)}, u32[]{:S(2)}) collective-permute-start(bf16[64,1024]{1,0:T(8,128)(2,1)S(1)} %collective-permute-done.11), channel_id=1, source_target_pairs={{8,0},{16,8},{24,16},{32,24},{40,32},{48,40},{56,48},{64,56},{72,6... | collective-permute-start | bytes 393224 | tf_op jit(solution)/shard_map/ppermute | solution.py:34
  102.7 8.6 %collective-permute-start.6 = (bf16[64,1024]{1,0:T(8,128)(2,1)}, bf16[64,1024]{1,0:T(8,128)(2,1)}, u32[]{:S(2)}, u32[]{:S(2)}) collective-permute-start(bf16[64,1024]{1,0:T(8,128)(2,1)} %collective-permute-done.5), channel_id=1, source_target_pairs={{0,8},{8,16},{16,24},{24,32},{32,40},{40,48},{48,56},{56,64},{64,7... | collective-permute-start | bytes 393224 | tf_op jit(solution)/shard_map/ppermute | solution.py:30
  102.7 9.4 %collective-permute-start.13 = (bf16[64,1024]{1,0:T(8,128)(2,1)}, bf16[64,1024]{1,0:T(8,128)(2,1)}, u32[]{:S(2)}, u32[]{:S(2)}) collective-permute-start(bf16[64,1024]{1,0:T(8,128)(2,1)} %collective-permute-done.12), channel_id=1, source_target_pairs={{8,0},{16,8},{24,16},{32,24},{40,32},{48,40},{56,48},{64,56},{72,6... | collective-permute-start | bytes 393224 | tf_op jit(solution)/shard_map/ppermute | solution.py:34
  111.3 8.6 %collective-permute-start.7 = (bf16[64,1024]{1,0:T(8,128)(2,1)}, bf16[64,1024]{1,0:T(8,128)(2,1)}, u32[]{:S(2)}, u32[]{:S(2)}) collective-permute-start(bf16[64,1024]{1,0:T(8,128)(2,1)} %collective-permute-done.6), channel_id=1, source_target_pairs={{0,8},{8,16},{16,24},{24,32},{32,40},{40,48},{48,56},{56,64},{64,7... | collective-permute-start | bytes 393224 | tf_op jit(solution)/shard_map/ppermute | solution.py:30
  112.0 19.9 %copy-start.6 = (bf16[64,1024]{1,0:T(8,128)(2,1)S(1)}, bf16[64,1024]{1,0:T(8,128)(2,1)}, u32[]{:S(2)}) copy-start(bf16[64,1024]{1,0:T(8,128)(2,1)} %copy-done.5) | copy-start | bytes 393220
  112.1 20.5 %copy-start.9 = (bf16[64,1024]{1,0:T(8,128)(2,1)S(1)}, bf16[64,1024]{1,0:T(8,128)(2,1)}, u32[]{:S(2)}) copy-start(bf16[64,1024]{1,0:T(8,128)(2,1)} %copy-done.8) | copy-start | bytes 393220
  112.1 21.2 %copy-start.11 = (bf16[64,1024]{1,0:T(8,128)(2,1)S(1)}, bf16[64,1024]{1,0:T(8,128)(2,1)}, u32[]{:S(2)}) copy-start(bf16[64,1024]{1,0:T(8,128)(2,1)} %copy-done.10) | copy-start | bytes 393220
  112.1 24.9 %collective-permute-start.14 = (bf16[64,1024]{1,0:T(8,128)(2,1)}, bf16[64,1024]{1,0:T(8,128)(2,1)S(1)}, u32[]{:S(2)}, u32[]{:S(2)}) collective-permute-start(bf16[64,1024]{1,0:T(8,128)(2,1)} %collective-permute-done.13), channel_id=1, source_target_pairs={{8,0},{16,8},{24,16},{32,24},{40,32},{48,40},{56,48},{64,56},{72,6... | collective-permute-start | bytes 393224 | tf_op jit(solution)/shard_map/ppermute | solution.py:34
  145.7 53.9 %copy-start.14 = (bf16[64,448]{1,0:T(8,128)(2,1)S(1)}, bf16[64,448]{1,0:T(8,128)(2,1)}, u32[]{:S(2)}) copy-start(bf16[64,448]{1,0:T(8,128)(2,1)} %param.24) | copy-start | bytes 172036
  145.7 55.7 %copy-start.17 = (bf16[7168]{0:T(1024)(128)(2,1)S(1)}, bf16[7168]{0:T(1024)(128)(2,1)}, u32[]{:S(2)}) copy-start(bf16[7168]{0:T(1024)(128)(2,1)} %param.25) | copy-start | bytes 43012
  145.7 53.9 %reduce-scatter.7.cloned.1.call-start = ((), (), s32[]{:S(2)}) async-start(), calls=%async_computation.9 | async-start | bytes 1179648 | tf_op jit(solution)/shard_map/reduce_scatter | solution.py:149
  159.8 167.7 %all-gather.4.cloned.1.call-start = ((), (), s32[]{:S(2)}) async-start(), calls=%async_computation.7 | async-start | bytes 16842752 | tf_op jit(solution)/shard_map/all_gather | solution.py:162
  201.2 230.3 %all-gather.6.cloned.1.call-start = ((), (), s32[]{:S(2)}) async-start(), calls=%async_computation.8 | async-start | bytes 2785280 | tf_op jit(solution)/shard_map/all_gather | solution.py:179
  383.7 6.8 %copy-start.1 = (bf16[640,7168]{1,0:T(8,128)(2,1)S(1)}, bf16[640,7168]{1,0:T(8,128)(2,1)}, u32[]{:S(2)}) copy-start(bf16[640,7168]{1,0:T(8,128)(2,1)} %convert_element_type.97) | copy-start | bytes 27525124
  383.8 7.2 %copy-start.20 = (bf16[1,7168,128]{2,1,0:T(8,128)(2,1)S(1)}, bf16[1,7168,128]{2,1,0:T(8,128)(2,1)}, u32[]{:S(2)}) copy-start(bf16[1,7168,128]{2,1,0:T(8,128)(2,1)} %param.30) | copy-start | bytes 5505028
  436.1 3.4 copy-start.3
  444.7 32.7 %copy-start.18 = (f32[64,8]{0,1:T(8,128)S(1)}, f32[64,8]{0,1:T(8,128)}, u32[]{:S(2)}) copy-start(f32[64,8]{0,1:T(8,128)} %param.27) | copy-start | bytes 6148
  444.7 44.9 %copy-start.4 = (bf16[64,448]{1,0:T(8,128)(2,1)S(1)}, bf16[64,448]{1,0:T(8,128)(2,1)}, u32[]{:S(2)}) copy-start(bf16[64,448]{1,0:T(8,128)(2,1)} %add_convert_fusion) | copy-start | bytes 172036
  470.5 19.0 %all-to-all-start.3 = ((bf16[16,40,448]{2,1,0:T(8,128)(2,1)}), bf16[16,40,448]{2,1,0:T(8,128)(2,1)S(1)}, u32[]{:S(2)}, u32[]{:S(2)}) async-start(bf16[16,40,448]{2,1,0:T(8,128)(2,1)} %all_to_all.46), calls=%async_computation.4 | async-start | bytes 1310720 | tf_op jit(solution)/shard_map/all_to_all | solution.py:196
Sparse Core Ops, SparseCore 0:
  145.8 11.3 reduce-scatter.4
  159.9 39.6 reduce-scatter.6
  203.2 124.1 all-gather.3
  394.3 37.1 all-gather.5
